TPU v7x, 32 devices: a whole 2x2x4 slice. The times are simulated.
32 devices in a mesh: req: 2 (over x), seq: 16 (over z, y, core).
Axes of the slice: x: 2, y: 2, z: 4, core: 2. Of those that a mesh axis runs over, the one named last changes fastest.
Arguments:
- states: bfloat16 [4, 4, 4544], P(None, 'req', 'seq'), may hold values from -6 to 6
- kv_cache: bfloat16 [4, 8192, 128], P('req', 'seq'), may hold values from -48 to 48, as said below
- lengths: int32 [4], replicated, may hold values from 1 to 8188, as said below
- placement: int32 [4], replicated, may hold values from 0 to 3, each once
- norm_gain: bfloat16 [4544], replicated, may hold values from 0.25 to 1.75
- norm_bias: bfloat16 [4544], replicated, may hold values from -1.5 to 1.5
- w_query: bfloat16 [4544, 4544], P('req', 'seq'), may hold values from -0.09375 to 0.09375
- w_keyval: bfloat16 [4544, 128], P('req'), may hold values from -0.09375 to 0.09375
- w_out: bfloat16 [4544, 4544], P('seq', 'req'), may hold values from -0.09375 to 0.09375
- w_up: bfloat16 [4544, 18176], P('req', 'seq'), may hold values from -0.09375 to 0.09375
- w_down: bfloat16 [18176, 4544], P('seq', 'req'), may hold values from -0.046875 to 0.046875
Outputs:
- new_states: bfloat16 [4, 4, 4544], P(None, 'req', 'seq')
- new_cache: bfloat16 [4, 8192, 128], P('req', 'seq')
Inputs may be any that keep to these rules, and one draw needn't show every extreme that they name: Request r's cache holds its first lengths[r] positions; some request has exactly 8188. `kv_cache`: row i is the cache of request placement[i]; positions at or beyond that request's length hold arbitrary values. `placement`: each request is served by exactly one slot.
All inputs are finite; a program needn't handle non-finite values.
Results may differ from a plain program's by a relative error of at most 0.012.
The roundings to bfloat16 on the way count: a program that leaves them out, or rounds other values in their place, can miss the bound.
Values may be sent and summed in bfloat16 or wider, within the bound.
No kernel may reach another device: no remote copies, remote signals or barrier semaphores. Data moves between devices by JAX's collectives and lax.ppermute only.
A program may use at most 192 MiB of HBM per device.

v0:
```python
import jax
import jax.numpy as jnp
from jax import lax
from jax.sharding import PartitionSpec as P

EPSILON = 1e-05
NEGATIVE = -1e30
ALL = ("req", "seq")


def layer_norm(row_block, norm_gain, norm_bias):
    values = row_block.astype(jnp.float32)
    average = jnp.mean(values, axis=-1, keepdims=True)
    centered = values - average
    spread = jnp.mean(centered * centered, axis=-1, keepdims=True)
    scaled = centered * lax.rsqrt(spread + EPSILON)
    return (scaled * norm_gain.astype(jnp.float32) + norm_bias.astype(jnp.float32)).astype(
        jnp.bfloat16
    )


def rotate(vectors, positions):
    head_width = vectors.shape[-1]
    half_width = head_width // 2
    frequency = 10000.0 ** (-(jnp.arange(half_width, dtype=jnp.float32) * 2.0) / head_width)
    angles = positions.astype(jnp.float32)[:, None] * frequency[None, :]
    cosine = jnp.concatenate([jnp.cos(angles), jnp.cos(angles)], axis=-1)[:, None, :]
    sine_wave = jnp.concatenate([jnp.sin(angles), jnp.sin(angles)], axis=-1)[:, None, :]
    turned = jnp.concatenate([-vectors[..., half_width:], vectors[..., :half_width]], axis=-1)
    return vectors * cosine + turned * sine_wave


def shards(
    states,
    kv_cache,
    lengths,
    placement,
    norm_gain,
    norm_bias,
    w_query,
    w_keyval,
    w_out,
    w_up,
    w_down,
):
    steps = states.shape[0]
    group_rows = kv_cache.shape[0]
    seg_length = kv_cache.shape[1]
    head_width = kv_cache.shape[2] // 2
    model_width = norm_gain.shape[0]
    head_count = model_width // head_width
    slice_width = states.shape[2]
    part_width = w_query.shape[0]
    total = placement.shape[0]
    req_size = total // group_rows
    seq_size = model_width // slice_width
    rows = steps * total
    group_index = lax.axis_index("req")
    shard_index = lax.axis_index("seq")
    own_requests = lax.dynamic_slice_in_dim(placement, group_index * group_rows, group_rows, 0)
    slot_lengths = jnp.take(lengths, own_requests)
    step_offsets = jnp.arange(steps, dtype=jnp.int32)
    positions = slot_lengths[None, :] + step_offsets[:, None]
    every = lax.all_gather(states, ALL, axis=0, tiled=False)
    every = every.reshape(req_size, seq_size, steps, group_rows, slice_width)
    every = every.transpose(2, 0, 3, 1, 4).reshape(steps, total, model_width)
    current_all = jnp.take(every, placement, axis=1)
    normed = layer_norm(current_all.reshape(rows, model_width), norm_gain, norm_bias)
    normed_part = lax.dynamic_slice_in_dim(normed, group_index * part_width, part_width, 1)
    part_query = jnp.dot(normed_part, w_query, preferred_element_type=jnp.float32)
    part_keyval = jnp.dot(normed_part, w_keyval, preferred_element_type=jnp.float32)
    part_up = jnp.dot(normed_part, w_up, preferred_element_type=jnp.float32)
    first = lax.psum(jnp.concatenate([part_query, part_keyval, part_up], axis=1), "req")
    query_raw = first[:, :slice_width].astype(jnp.bfloat16).reshape(steps, total, slice_width)
    keyval = first[:, slice_width : slice_width + 2 * head_width].reshape(
        steps, total, 2 * head_width
    )
    up_part = first[:, slice_width + 2 * head_width :]
    own_query = lax.dynamic_slice_in_dim(query_raw, group_index * group_rows, group_rows, 1)
    query_all = lax.all_gather(own_query, "seq", axis=2, tiled=True)
    flat_positions = positions.reshape(-1)
    query_rows = rotate(
        query_all.astype(jnp.float32).reshape(steps * group_rows, head_count, head_width),
        flat_positions,
    ).astype(jnp.bfloat16)
    own_keyval = lax.dynamic_slice_in_dim(keyval, group_index * group_rows, group_rows, 1)
    own_keyval = own_keyval.reshape(steps * group_rows, 2 * head_width)
    new_key = rotate(own_keyval[:, None, :head_width], flat_positions)[:, 0, :]
    new_entry = jnp.concatenate([new_key, own_keyval[:, head_width:]], axis=-1).astype(jnp.bfloat16)
    new_entry = new_entry.reshape(steps, group_rows, 2 * head_width)
    local_slots = jnp.arange(seg_length, dtype=jnp.int32)
    global_positions = shard_index * seg_length + local_slots
    cache_now = kv_cache
    for step_index in range(steps):
        write_mask = global_positions[None, :] == positions[step_index][:, None]
        cache_now = jnp.where(write_mask[:, :, None], new_entry[step_index][:, None, :], cache_now)
    key_rows = cache_now[:, :, :head_width]
    value_rows = cache_now[:, :, head_width:]
    query_heads = (
        query_rows.reshape(steps, group_rows, head_count, head_width)
        .transpose(1, 0, 2, 3)
        .reshape(group_rows, steps * head_count, head_width)
    )
    scores = jnp.einsum(
        "gqd,gsd->gqs", query_heads, key_rows, preferred_element_type=jnp.float32
    ) * head_width ** (-0.5)
    valid = global_positions[None, None, :] <= positions.T[:, :, None]
    valid = jnp.broadcast_to(
        valid[:, :, None, :], (group_rows, steps, head_count, seg_length)
    ).reshape(group_rows, steps * head_count, seg_length)
    local_peak = jnp.max(jnp.where(valid, scores, NEGATIVE), axis=-1)
    weights = jnp.where(valid, jnp.exp(scores - local_peak[:, :, None]), 0.0)
    local_total = jnp.sum(weights, axis=-1)
    local_weighted = jnp.einsum(
        "gqs,gsd->gqd", weights, value_rows, preferred_element_type=jnp.float32
    )
    peak_buffer = jnp.full((total, steps * head_count), NEGATIVE, jnp.float32)
    peak_buffer = lax.dynamic_update_slice_in_dim(
        peak_buffer, local_peak, group_index * group_rows, 0
    )
    peak = lax.pmax(peak_buffer, ALL)
    own_peak = lax.dynamic_slice_in_dim(peak, group_index * group_rows, group_rows, 0)
    scale = jnp.exp(local_peak - own_peak)
    packed = jnp.concatenate(
        [local_weighted * scale[:, :, None], (local_total * scale)[:, :, None]], axis=-1
    )
    packed_buffer = jnp.zeros((total, steps * head_count, head_width + 1), jnp.float32)
    packed_buffer = lax.dynamic_update_slice_in_dim(
        packed_buffer, packed, group_index * group_rows, 0
    )
    summed = lax.psum(packed_buffer, ALL)
    mixed = summed[:, :, :head_width] / summed[:, :, head_width:]
    mixed = (
        mixed.reshape(total, steps, model_width)
        .transpose(1, 0, 2)
        .reshape(rows, model_width)
        .astype(jnp.bfloat16)
    )
    mixed_part = lax.dynamic_slice_in_dim(mixed, shard_index * slice_width, slice_width, 1)
    hidden = jax.nn.gelu(up_part, approximate=False).astype(jnp.bfloat16)
    partial_sum = jnp.dot(mixed_part, w_out, preferred_element_type=jnp.float32) + jnp.dot(
        hidden, w_down, preferred_element_type=jnp.float32
    )
    out_buffer = jnp.zeros((rows, model_width), jnp.float32)
    out_buffer = lax.dynamic_update_slice_in_dim(
        out_buffer, partial_sum, group_index * part_width, 1
    )
    branch = lax.psum(out_buffer, ALL).reshape(steps, total, model_width)
    inverse = jnp.zeros((total,), jnp.int32).at[placement].set(jnp.arange(total, dtype=jnp.int32))
    own_inverse = lax.dynamic_slice_in_dim(inverse, group_index * group_rows, group_rows, 0)
    own_branch = jnp.take(branch, own_inverse, axis=1)
    own_branch = lax.dynamic_slice_in_dim(own_branch, shard_index * slice_width, slice_width, 2)
    new_states = (states.astype(jnp.float32) + own_branch).astype(jnp.bfloat16)
    return (new_states, cache_now)


def solution(mesh):
    in_specs = (
        P(None, "req", "seq"),
        P("req", "seq", None),
        P(),
        P(),
        P(),
        P(),
        P("req", "seq"),
        P("req", None),
        P("seq", "req"),
        P("req", "seq"),
        P("seq", "req"),
    )
    out_specs = (P(None, "req", "seq"), P("req", "seq", None))
    return jax.shard_map(shards, mesh=mesh, in_specs=in_specs, out_specs=out_specs, check_vma=False)
```

profile of v0, /device:TPU:8, one launch (start us, length us, event | category | flops | bytes accessed | tf_op | source)
XLA Modules:
  0.0 437.4 jit_solution(13402356280962080718)
XLA Ops:
  7.2 0.8 compare_select_fusion.2
  8.0 0.7 compare_and_fusion
  8.6 0.8 dynamic-slice.1
  9.4 0.8 dynamic-slice.2
  10.2 38.8 %all-gather = bf16[128,2,284]{2,1,0:T(2,128)(2,1)S(1)} all-gather(bf16[4,2,284]{2,1,0:T(2,128)(2,1)} %param.11), channel_id=2, replica_groups=mesh['req'=2,'seq'=16] {'req','seq'}, dimensions={0}, use_global_device_ids=true | all-gather | bytes 149952 | tf_op jit(solution)/shard_map/all_gather | solution.py:64
  49.4 0.7 gather_fusion.1
  51.3 3.5 fusion.96
  55.5 0.8 concatenate.40
  58.3 19.3 %all-reduce.4.cloned.1.call-done = f32[16,1548]{1,0:T(8,128)} async-done(((f32[16,1548]{1,0:T(8,128)}), f32[16,1548]{1,0:T(8,128)}) %all-reduce.4.cloned.1.call-update) | async-done | bytes 99088 | tf_op jit(solution)/shard_map/psum | solution.py:73
  77.6 0.8 slice.99
  78.4 0.7 slice.124
  79.4 32.2 %all_gather.11 = bf16[4,2,4544]{0,1,2:T(2,128)(2,1)} all-gather(bf16[4,2,284]{0,1,2:T(2,128)(2,1)S(1)} %copy.88), channel_id=1, replica_groups=mesh['req'=2,'seq'=16] {'seq'}, dimensions={2}, use_global_device_ids=true | all-gather | bytes 77248 | tf_op jit(solution)/shard_map/all_gather | solution.py:80
  111.6 5.2 %copy.73 = bf16[4,2,4544]{2,0,1:T(4,128)(2,1)S(1)} copy(bf16[4,2,4544]{0,1,2:T(2,128)(2,1)} %all_gather.11) | data formatting | bytes 145408 | tf_op jit(solution)/shard_map/all_gather | solution.py:80
  119.3 41.3 %pmax.7 = f32[4,284]{1,0:T(4,128)S(1)} all-reduce(f32[4,284]{1,0:T(4,128)S(1)} %constant_dynamic-update-slice_fusion.1), channel_id=1, replica_groups=mesh['req'=2,'seq'=16] {'req','seq'}, use_global_device_ids=true, to_apply=%region_5.6 | all-reduce | flops 1136 | bytes 9088 | tf_op jit(solution)/shard_map/pmax | solution.py:121
  161.7 0.8 copy-done.2
  163.2 129.3 %all-reduce.6.cloned.1.call-done = f32[4,284,65]{2,1,0:T(8,128)} async-done(((f32[4,284,65]{2,1,0:T(8,128)}), f32[4,284,65]{2,1,0:T(8,128)}) %all-reduce.6.cloned.1.call-update) | async-done | bytes 295376 | tf_op jit(solution)/shard_map/psum | solution.py:131
  292.5 1.5 slice_reduce_fusion
  294.0 1.3 fusion.1
  296.2 3.4 convolution_add_fusion
  299.7 1.3 dynamic_update_slice.11
  301.1 0.8 copy.84
  302.0 0.8 copy.86
  302.9 125.7 %all-reduce.8.cloned.1.call-done = f32[4,4,4544]{2,0,1:T(4,128)} async-done(((f32[4,4,4544]{2,0,1:T(4,128)}), f32[4,4,4544]{2,0,1:T(4,128)}) %all-reduce.8.cloned.1.call-update) | async-done | bytes 290832 | tf_op jit(solution)/shard_map/psum | solution.py:148
  428.5 1.6 gather_fusion.2
  (105 shorter events, 10.5 us)
Async XLA Ops:
  7.2 288.4 %copy-start = (bf16[284,2272]{1,0:T(8,128)(2,1)S(1)}, bf16[284,2272]{1,0:T(8,128)(2,1)}, u32[]{:S(2)}) copy-start(bf16[284,2272]{1,0:T(8,128)(2,1)} %param.19) | copy-start | bytes 3871492
  7.2 70.4 %all-reduce.4.cloned.1.call-start = ((), (), s32[]{:S(2)}) async-start(), calls=%async_computation | async-start | bytes 212992 | tf_op jit(solution)/shard_map/psum | solution.py:73
  51.3 3.5 copy-start.4
  51.3 3.8 copy-start.3
  54.8 1.6 copy-start.8
  54.8 1.7 copy-start.1
  55.1 2.6 copy-start.5
  56.3 236.2 %all-reduce.6.cloned.1.call-start = ((), (), s32[]{:S(2)}) async-start(), calls=%async_computation.1 | async-start | bytes 1179648 | tf_op jit(solution)/shard_map/psum | solution.py:131
  161.7 0.8 copy-start.2
  162.6 266.0 %all-reduce.8.cloned.1.call-start = ((), (), s32[]{:S(2)}) async-start(), calls=%async_computation.2 | async-start | bytes 589824 | tf_op jit(solution)/shard_map/psum | solution.py:148
  295.3 0.9 copy-start.6
  301.0 129.2 %copy-start.7 = (bf16[4,2,284]{2,1,0:T(2,128)(2,1)S(1)}, bf16[4,2,284]{2,1,0:T(2,128)(2,1)}, u32[]{:S(2)}) copy-start(bf16[4,2,284]{2,1,0:T(2,128)(2,1)} %param.11) | copy-start | bytes 13636
Sparse Core Ops, SparseCore 0:
  56.4 21.1 all-reduce.3
  162.7 129.7 all-reduce.5
  302.1 126.4 all-reduce.7
where the time goes:
time: 438 us; the launch traced here: 437 us
  waiting for transfers between devices  274 us (63%)
  blocking collectives  112 us (26%)
  local copies, waits for them, and re-layouts  22.3 us (5%)
  between operations  14.2 us (3%)
  matrix products  8.89 us (2%)
  other arithmetic  5.32 us (1%)
    psum x1, waiting for transfers between devices, shards(): summed = lax.psum(packed_buffer, ALL)  129 us
    psum x1, waiting for transfers between devices, shards(): branch = lax.psum(out_buffer, ALL).reshape(steps, total, model_width)  126 us
    pmax x1, blocking collectives, shards(): peak = lax.pmax(peak_buffer, ALL)  41.3 us
    all_gather x1, blocking collectives, shards(): every = lax.all_gather(states, ALL, axis=0, tiled=False)  38.8 us
    all_gather x1, blocking collectives, shards(): query_all = lax.all_gather(own_query, 'seq', axis=2, tiled=True)  32.2 us
    psum x1, waiting for transfers between devices, shards(): lax.psum(jnp.concatenate([part_query, part_keyval, part_up], axis=1), 'req')  19.3 us
  transfers between devices with their start and end apart: 3, of which 3 were waited for; matrix products, arithmetic and copies ran while one was open for 1% of the time, Pallas kernels for 0%

commit v1 on v0

--- a/solution.py
+++ b/solution.py
@@ -145,7 +145,7 @@
     out_buffer = lax.dynamic_update_slice_in_dim(
         out_buffer, partial_sum, group_index * part_width, 1
     )
-    branch = lax.psum(out_buffer, ALL).reshape(steps, total, model_width)
+    branch = lax.psum(lax.psum(out_buffer, "seq"), "req").reshape(steps, total, model_width)
     inverse = jnp.zeros((total,), jnp.int32).at[placement].set(jnp.arange(total, dtype=jnp.int32))
     own_inverse = lax.dynamic_slice_in_dim(inverse, group_index * group_rows, group_rows, 0)
     own_branch = jnp.take(branch, own_inverse, axis=1)

time: 438 us -> 427 us (0.975)
  waiting for transfers between devices: 274 us -> 260 us
    psum x1 -> x2, waiting for transfers between devices: 126 us -> 111 us  [the longest x1 89.2 us: shards(): lax.psum(out_buffer, 'seq')]
  transfers between devices with their start and end apart: 3 -> 4, of which waited for: 3 -> 4; matrix products, arithmetic and copies ran while one was open for 1% -> 1% of each run, Pallas kernels for 0% -> 0%
where the time goes in v1:
time: 427 us; the launch traced here: 425 us
  waiting for transfers between devices  260 us (61%)
  blocking collectives  112 us (26%)
  local copies, waits for them, and re-layouts  24 us (6%)
  between operations  14.2 us (3%)
  matrix products  8.89 us (2%)
  other arithmetic  5.32 us (1%)
    psum x1, waiting for transfers between devices, shards(): summed = lax.psum(packed_buffer, ALL)  130 us
    psum x1, waiting for transfers between devices, shards(): lax.psum(out_buffer, 'seq')  89.2 us
    pmax x1, blocking collectives, shards(): peak = lax.pmax(peak_buffer, ALL)  41.3 us
    all_gather x1, blocking collectives, shards(): every = lax.all_gather(states, ALL, axis=0, tiled=False)  38.8 us
    all_gather x1, blocking collectives, shards(): query_all = lax.all_gather(own_query, 'seq', axis=2, tiled=True)  32.2 us
    psum x1, waiting for transfers between devices, shards(): lax.psum(lax.psum(out_buffer, 'seq'), 'req')  21.5 us
    psum x1, waiting for transfers between devices, shards(): lax.psum(jnp.concatenate([part_query, part_keyval, part_up], axis=1), 'req')  19.3 us
  transfers between devices with their start and end apart: 4, of which 4 were waited for; matrix products, arithmetic and copies ran while one was open for 1% of the time, Pallas kernels for 0%

profile of v1, /device:TPU:8, one launch (start us, length us, event | category | flops | bytes accessed | tf_op | source)
XLA Modules:
  0.0 424.8 jit_solution(7119558214725713767)
XLA Ops:
  7.2 0.8 compare_select_fusion.2
  8.6 0.8 dynamic-slice.1
  9.4 0.8 dynamic-slice.2
  10.2 38.8 %all-gather = bf16[128,2,284]{2,1,0:T(2,128)(2,1)S(1)} all-gather(bf16[4,2,284]{2,1,0:T(2,128)(2,1)} %param.11), channel_id=2, replica_groups=mesh['req'=2,'seq'=16] {'req','seq'}, dimensions={0}, use_global_device_ids=true | all-gather | bytes 149952 | tf_op jit(solution)/shard_map/all_gather | solution.py:64
  51.3 3.5 fusion.96
  55.5 0.8 concatenate.40
  58.3 19.3 %all-reduce.5.cloned.1.call-done = f32[16,1548]{1,0:T(8,128)} async-done(((f32[16,1548]{1,0:T(8,128)}), f32[16,1548]{1,0:T(8,128)}) %all-reduce.5.cloned.1.call-update) | async-done | bytes 99088 | tf_op jit(solution)/shard_map/psum | solution.py:73
  77.6 0.8 slice.99
  78.4 0.7 slice.124
  79.4 32.2 %all_gather.11 = bf16[4,2,4544]{0,1,2:T(2,128)(2,1)} all-gather(bf16[4,2,284]{0,1,2:T(2,128)(2,1)S(1)} %copy.88), channel_id=1, replica_groups=mesh['req'=2,'seq'=16] {'seq'}, dimensions={2}, use_global_device_ids=true | all-gather | bytes 77248 | tf_op jit(solution)/shard_map/all_gather | solution.py:80
  111.6 5.2 %copy.73 = bf16[4,2,4544]{2,0,1:T(4,128)(2,1)S(1)} copy(bf16[4,2,4544]{0,1,2:T(2,128)(2,1)} %all_gather.11) | data formatting | bytes 145408 | tf_op jit(solution)/shard_map/all_gather | solution.py:80
  119.3 41.3 %pmax.7 = f32[4,284]{1,0:T(4,128)S(1)} all-reduce(f32[4,284]{1,0:T(4,128)S(1)} %constant_dynamic-update-slice_fusion.1), channel_id=1, replica_groups=mesh['req'=2,'seq'=16] {'req','seq'}, use_global_device_ids=true, to_apply=%region_5.6 | all-reduce | flops 1136 | bytes 9088 | tf_op jit(solution)/shard_map/pmax | solution.py:121
  161.7 0.8 copy-done.2
  162.6 129.9 %all-reduce.7.cloned.1.call-done = f32[4,284,65]{2,1,0:T(8,128)} async-done(((f32[4,284,65]{2,1,0:T(8,128)}), f32[4,284,65]{2,1,0:T(8,128)}) %all-reduce.7.cloned.1.call-update) | async-done | bytes 295376 | tf_op jit(solution)/shard_map/psum | solution.py:131
  292.5 1.5 slice_reduce_fusion
  294.0 1.3 fusion.1
  296.2 3.4 convolution_add_fusion
  299.7 1.3 dynamic_update_slice.11
  301.8 89.2 %all-reduce.9.cloned.1.call-done = f32[16,4544]{1,0:T(8,128)} async-done(((f32[16,4544]{1,0:T(8,128)}), f32[16,4544]{1,0:T(8,128)}) %all-reduce.9.cloned.1.call-update) | async-done | bytes 290832 | tf_op jit(solution)/shard_map/psum | solution.py:148
  391.0 1.0 reshape.355
  392.1 0.8 copy.84
  393.6 0.8 copy.86
  394.4 21.5 %all-reduce.11.cloned.1.call-done = f32[4,4,4544]{2,0,1:T(4,128)} async-done(((f32[4,4,4544]{2,0,1:T(4,128)}), f32[4,4,4544]{2,0,1:T(4,128)}) %all-reduce.11.cloned.1.call-update) | async-done | bytes 290832 | tf_op jit(solution)/shard_map/psum | solution.py:148
  416.0 1.6 gather_fusion.2
  (110 shorter events, 12.5 us)
Async XLA Ops:
  7.2 288.5 %copy-start = (bf16[284,2272]{1,0:T(8,128)(2,1)S(1)}, bf16[284,2272]{1,0:T(8,128)(2,1)}, u32[]{:S(2)}) copy-start(bf16[284,2272]{1,0:T(8,128)(2,1)} %param.19) | copy-start | bytes 3871492
  7.2 70.4 %all-reduce.5.cloned.1.call-start = ((), (), s32[]{:S(2)}) async-start(), calls=%async_computation | async-start | bytes 212992 | tf_op jit(solution)/shard_map/psum | solution.py:73
  51.3 3.5 copy-start.5
  51.3 3.8 copy-start.3
  54.8 1.6 copy-start.9
  54.8 1.7 copy-start.1
  55.1 2.6 copy-start.6
  56.3 236.2 %all-reduce.7.cloned.1.call-start = ((), (), s32[]{:S(2)}) async-start(), calls=%async_computation.1 | async-start | bytes 1179648 | tf_op jit(solution)/shard_map/psum | solution.py:131
  161.7 0.8 copy-start.2
  162.6 228.4 %all-reduce.9.cloned.1.call-start = ((), (), s32[]{:S(2)}) async-start(), calls=%async_computation.2 | async-start | bytes 589824 | tf_op jit(solution)/shard_map/psum | solution.py:148
  295.3 0.9 copy-start.7
  301.0 0.7 copy-start.4
  301.7 115.8 %copy-start.8 = (bf16[4,2,284]{2,1,0:T(2,128)(2,1)S(1)}, bf16[4,2,284]{2,1,0:T(2,128)(2,1)}, u32[]{:S(2)}) copy-start(bf16[4,2,284]{2,1,0:T(2,128)(2,1)} %param.11) | copy-start | bytes 13636
  301.7 114.2 %all-reduce.11.cloned.1.call-start = ((), (), s32[]{:S(2)}) async-start(), calls=%async_computation.3 | async-start | bytes 589824 | tf_op jit(solution)/shard_map/psum | solution.py:148
Sparse Core Ops, SparseCore 0:
  56.4 21.1 all-reduce.4
  162.7 129.7 all-reduce.6
  301.9 89.1 all-reduce.8
  393.2 22.6 all-reduce.10
